TPU v7x, 256 devices: a whole 4x4x8 slice. The times are simulated.
256 devices in a mesh: dp: 32 (over x, y, core), mp: 8 (over z).
Axes of the slice: x: 4, y: 4, z: 8, core: 2. Of those that a mesh axis runs over, the one named last changes fastest.
Arguments:
- hidden: bfloat16 [512, 1024], P('dp'), may hold values from -6 to 6
- attn_gain: float32 [1024], replicated, may hold values from 0.25 to 1.75
- w_qkv: bfloat16 [1024, 3, 1024], P(None, None, 'mp'), may hold values from -2 to 2
- w_out: bfloat16 [1024, 1024], P('mp'), may hold values from -0.1875 to 0.1875
- mlp_gain: float32 [1024], replicated, may hold values from 0.25 to 1.75
- w_gate_up: bfloat16 [1024, 2, 4096], P(None, None, 'mp'), may hold values from -0.1875 to 0.1875
- w_down: bfloat16 [4096, 1024], P('mp'), may hold values from -0.09375 to 0.09375
- kv_cache: bfloat16 [2, 4096, 128, 1024], P(None, 'dp', None, 'mp'), may hold values from -9 to 9
- lengths: int32 [512], replicated, may hold values from 1 to 16384, as said below
- page_request: int32 [4096], P('dp'), may hold values from -1 to 511, as said below
- page_index: int32 [4096], P('dp'), may hold values from 0 to 127, as said below
Outputs:
- appended: bfloat16 [2, 512, 1024], P(None, 'dp', 'mp')
- hidden_out: bfloat16 [512, 1024], P('dp')
Inputs may be any that keep to these rules, and one draw needn't show every extreme that they name: `lengths`: 4 requests hold exactly 16384 tokens, the others fewer than 512. `page_request`: each request owns exactly ceil(lengths / 128) pool pages, which may lie on any data devices; -1 marks an empty page. `page_index`: the pages of a request carry the places 0 to ceil(lengths / 128) - 1, each once; empty pages carry 0.
All inputs are finite; a program needn't handle non-finite values.
Results may differ from a plain program's by a relative error of at most 0.0085.
Values may be sent and summed in bfloat16 or wider, within the bound.
No kernel may reach another device: no remote copies, remote signals or barrier semaphores. Data moves between devices by JAX's collectives and lax.ppermute only.
A program may use at most 128 MiB of HBM per device.

v0:
```python
import jax
import jax.numpy as jnp
from jax import lax
from jax.sharding import PartitionSpec as P

HEAD_DIM = 64
PAGE_BLOCK = 8
EPSILON = 1e-05
NEGATIVE = -1e30


def merged_2(value, axis, join):
    pieces = jax.tree.map(lambda part: lax.all_gather(part, axis), value)
    head = jax.tree.map(lambda part: part[0], pieces)
    tail = jax.tree.map(lambda part: part[1:], pieces)
    running, _ = lax.scan(lambda running, piece: (join(running, piece), None), head, tail)
    return running


def rms_norm(values, gain):
    widened = values.astype(jnp.float32)
    mean_square = jnp.mean(widened * widened, axis=-1, keepdims=True)
    return (widened * lax.rsqrt(mean_square + EPSILON) * gain).astype(jnp.bfloat16)


def combine(first, second):
    largest = jnp.maximum(first[0], second[0])
    shrink_first = jnp.exp(first[0] - largest)
    shrink_second = jnp.exp(second[0] - largest)
    totals = first[1] * shrink_first + second[1] * shrink_second
    weighted = first[2] * shrink_first[:, :, None] + second[2] * shrink_second[:, :, None]
    return (largest, totals, weighted)


def body(
    hidden,
    attn_gain,
    w_qkv,
    w_out,
    mlp_gain,
    w_gate_up,
    w_down,
    kv_cache,
    lengths,
    page_request,
    page_index,
):
    local_rows = hidden.shape[0]
    head_cols = w_qkv.shape[2]
    local_heads = head_cols // HEAD_DIM
    pool_pages = kv_cache.shape[1]
    page_len = kv_cache.shape[2]
    data_devices = lax.axis_size("dp")
    requests = local_rows * data_devices
    score_scale = HEAD_DIM ** (-0.5)
    normed = rms_norm(hidden, attn_gain)
    projected = jnp.dot(
        normed, w_qkv.reshape(w_qkv.shape[0], 3 * head_cols), preferred_element_type=jnp.float32
    )
    projected = lax.optimization_barrier(projected.astype(jnp.bfloat16)).reshape(
        local_rows, 3, head_cols
    )
    appended = jnp.stack([projected[:, 1], projected[:, 2]])
    every_query = lax.all_gather(projected[:, 0], "dp", axis=0, tiled=True)
    own_queries = projected[:, 0].reshape(local_rows, local_heads, HEAD_DIM).astype(jnp.float32)
    own_keys = projected[:, 1].reshape(local_rows, local_heads, HEAD_DIM).astype(jnp.float32)
    own_values = projected[:, 2].reshape(local_rows, local_heads, HEAD_DIM).astype(jnp.float32)
    self_scores = jnp.sum(own_queries * own_keys, axis=-1) * score_scale
    home_row = lax.axis_index("dp") * local_rows
    start_max = lax.dynamic_update_slice(
        jnp.full((requests, local_heads), NEGATIVE, jnp.float32), self_scores, (home_row, 0)
    )
    start_totals = lax.dynamic_update_slice(
        jnp.zeros((requests, local_heads), jnp.float32),
        jnp.ones((local_rows, local_heads), jnp.float32),
        (home_row, 0),
    )
    start_weighted = lax.dynamic_update_slice(
        jnp.zeros((requests, local_heads, HEAD_DIM), jnp.float32), own_values, (home_row, 0, 0)
    )
    visit_order = jnp.arange(pool_pages, dtype=jnp.int32)
    trip_count = pool_pages // PAGE_BLOCK
    request_ids = jnp.arange(requests, dtype=jnp.int32)
    offsets = jnp.arange(page_len, dtype=jnp.int32)

    def visit(step_index, carry):
        running_max, totals, weighted = carry
        picked = lax.dynamic_slice_in_dim(visit_order, step_index * PAGE_BLOCK, PAGE_BLOCK, 0)
        fetched = jnp.take(kv_cache, picked, axis=1)
        owners = page_request[picked]
        page_pos = page_index[picked]
        clamped = jnp.maximum(owners, 0)
        chosen_queries = every_query[clamped].reshape(PAGE_BLOCK, local_heads, HEAD_DIM)
        key_rows = fetched[0].reshape(PAGE_BLOCK, page_len, local_heads, HEAD_DIM)
        value_rows = fetched[1].reshape(PAGE_BLOCK, page_len, local_heads, HEAD_DIM)
        scores = (
            jnp.einsum(
                "phd,pthd->pht", chosen_queries, key_rows, preferred_element_type=jnp.float32
            )
            * score_scale
        )
        position = page_pos[:, None] * page_len + offsets[None, :]
        usable = (owners[:, None] >= 0) & (position < lengths[clamped][:, None])
        page_max = jnp.max(jnp.where(usable[:, None, :], scores, NEGATIVE), axis=2)
        raw = jnp.where(usable[:, None, :], jnp.exp(scores - page_max[:, :, None]), 0.0)
        page_total = jnp.sum(raw, axis=2)
        page_sum = jnp.einsum(
            "pht,pthd->phd",
            raw.astype(jnp.bfloat16),
            value_rows,
            preferred_element_type=jnp.float32,
        )
        member = owners[:, None] == request_ids[None, :]
        candidate = jnp.max(jnp.where(member[:, :, None], page_max[:, None, :], NEGATIVE), axis=0)
        new_max = jnp.maximum(running_max, candidate)
        factors = jnp.where(owners[:, None] >= 0, jnp.exp(page_max - new_max[clamped]), 0.0)
        rescale = jnp.exp(running_max - new_max)
        onehot = member.astype(jnp.float32)
        totals = totals * rescale + jnp.einsum(
            "pr,ph->rh", onehot, page_total * factors, precision=lax.Precision.HIGHEST
        )
        weighted = weighted * rescale[:, :, None] + jnp.einsum(
            "pr,phd->rhd", onehot, page_sum * factors[:, :, None], precision=lax.Precision.HIGHEST
        )
        return (new_max, totals, weighted)

    running_max, totals, weighted = lax.fori_loop(
        0, trip_count, visit, (start_max, start_totals, start_weighted)
    )
    merged = merged_2((running_max, totals, weighted), "dp", combine)
    own_totals = lax.dynamic_slice_in_dim(merged[1], home_row, local_rows, 0)
    own_weighted = lax.dynamic_slice_in_dim(merged[2], home_row, local_rows, 0)
    context = (
        (own_weighted / own_totals[:, :, None]).reshape(local_rows, head_cols).astype(jnp.bfloat16)
    )
    attended = lax.psum(jnp.dot(context, w_out, preferred_element_type=jnp.float32), "mp")
    residual = lax.optimization_barrier(
        (hidden.astype(jnp.float32) + attended).astype(jnp.bfloat16)
    )
    normed_mlp = rms_norm(residual, mlp_gain)
    hidden_cols = w_gate_up.shape[2]
    gate_up = jnp.dot(
        normed_mlp,
        w_gate_up.reshape(w_gate_up.shape[0], 2 * hidden_cols),
        preferred_element_type=jnp.float32,
    ).reshape(local_rows, 2, hidden_cols)
    activated = (jax.nn.silu(gate_up[:, 0]) * gate_up[:, 1]).astype(jnp.bfloat16)
    lowered = lax.psum(jnp.dot(activated, w_down, preferred_element_type=jnp.float32), "mp")
    hidden_out = (residual.astype(jnp.float32) + lowered).astype(jnp.bfloat16)
    return (appended, hidden_out)


def solution(mesh):
    return jax.shard_map(
        body,
        mesh=mesh,
        in_specs=(
            P("dp", None),
            P(),
            P(None, None, "mp"),
            P("mp", None),
            P(),
            P(None, None, "mp"),
            P("mp", None),
            P(None, "dp", None, "mp"),
            P(),
            P("dp"),
            P("dp"),
        ),
        out_specs=(P(None, "dp", "mp"), P("dp", None)),
        check_vma=False,
    )
```

profile of v0, /device:TPU:2, one launch (start us, length us, event | category | flops | bytes accessed | tf_op | source)
XLA Modules:
  0.0 589.8 jit_solution(4555764252407409945)
XLA Ops:
  11.2 24.7 %all-gather = bf16[512,1,128]{2,0,1:T(8,128)(2,1)S(1)} all-gather(bf16[16,1,128]{2,0,1:T(8,128)(2,1)S(1)} %copy.113), channel_id=2, replica_groups=mesh['dp'=32,'mp'=8] {'dp'}, dimensions={0}, use_global_device_ids=true | all-gather | bytes 135168 | tf_op jit(solution)/shard_map/all_gather | solution.py:64
  36.7 190.9 %while.35 = (s32[]{:T(128)}, f32[512,2]{0,1:T(2,128)S(1)}, f32[512,2]{0,1:T(2,128)S(1)}, f32[512,2,64]{0,2,1:T(8,128)S(1)}, s32[128]{0:T(128)S(1)}, /*index=5*/s...) while((s32[]{:T(128)}, f32[512,2]{0,1:T(2,128)S(1)}, ...), condition=%wide.region_6.7_spmd.clone.clone, body=%wide.region_2.6_spmd.clone.clone.sunk | while | flops 7361630 | bytes 5361311 | solution.py:127
  41.5 4.0 gather_fusion.2
  53.5 4.0 gather_fusion.2
  65.4 4.0 gather_fusion.2
  77.3 4.0 gather_fusion.2
  89.3 4.0 gather_fusion.2
  101.2 4.0 gather_fusion.2
  113.1 4.0 gather_fusion.2
  125.1 4.0 gather_fusion.2
  137.0 4.0 gather_fusion.2
  148.9 4.0 gather_fusion.2
  160.9 4.0 gather_fusion.2
  172.8 4.0 gather_fusion.2
  184.7 4.0 gather_fusion.2
  220.5 4.0 gather_fusion.2
  228.4 22.8 %all-gather.1 = f32[16384,2]{0,1:T(2,128)S(1)} all-gather(f32[512,2]{0,1:T(2,128)S(1)} %get-tuple-element.259), channel_id=3, replica_groups=mesh['dp'=32,'mp'=8] {'dp'}, dimensions={0}, use_global_device_ids=true | all-gather | bytes 135168 | tf_op jit(solution)/shard_map/all_gather | solution.py:13
  251.2 24.6 %all-gather.2 = f32[16384,2]{0,1:T(2,128)S(1)} all-gather(f32[512,2]{0,1:T(2,128)S(1)} %get-tuple-element.260), channel_id=4, replica_groups=mesh['dp'=32,'mp'=8] {'dp'}, dimensions={0}, use_global_device_ids=true | all-gather | bytes 135168 | tf_op jit(solution)/shard_map/all_gather | solution.py:13
  275.8 12.0 %all-gather.6.cloned.1.call-done = f32[16384,2,64]{0,2,1:T(8,128)} async-done(((f32[512,2,64]{0,2,1:T(8,128)}), f32[16384,2,64]{0,2,1:T(8,128)}) %all-gather.6.cloned.1.call-update) | async-done | bytes 8388624 | tf_op jit(solution)/shard_map/all_gather | solution.py:13
  289.0 7.1 %slice.95 = f32[15872,2,64]{0,2,1:T(8,128)} slice(f32[16384,2,64]{0,2,1:T(8,128)} %all-gather.6.cloned.1.call-done), slice={[512:16384], [0:2], [0:64]} | slice | bytes 16252928 | tf_op jit(solution)/shard_map/slice | solution.py:15
  296.1 19.6 %copy.125 = f32[15872,2,64]{2,1,0:T(2,128)} copy(f32[15872,2,64]{0,2,1:T(8,128)} %slice.95) | data formatting | bytes 16252928 | tf_op jit(solution)/shard_map/while | solution.py:16
  315.7 119.1 %while.34 = (s32[]{:T(128)}, f32[512,2]{0,1:T(2,128)S(1)}, f32[512,2]{0,1:T(2,128)S(1)}, f32[512,2,64]{2,1,0:T(2,128)S(1)}, f32[31,512,2]{1,2,0:T(2,128)S(1)}, /...) while((s32[]{:T(128)}, f32[512,2]{0,1:T(2,128)S(1)}, f32[512,2]{0,1:T(2,128)S(1)}, ...), condition=%wide.region_8.9_spmd, body=%wide.region_7.8_spmd.sunk | while | flops 202754 | bytes 843877 | solution.py:16
  442.4 65.8 %all-reduce.3.cloned.1.call-done = f32[16,1024]{1,0:T(8,128)} async-done(((f32[16,1024]{1,0:T(8,128)}), f32[16,1024]{1,0:T(8,128)}) %all-reduce.3.cloned.1.call-update) | async-done | bytes 65552 | tf_op jit(solution)/shard_map/psum | solution.py:136
  511.4 70.4 %all-reduce.5.cloned.1.call-done = f32[16,1024]{1,0:T(8,128)} async-done(((f32[16,1024]{1,0:T(8,128)}), f32[16,1024]{1,0:T(8,128)}) %all-reduce.5.cloned.1.call-update) | async-done | bytes 65552 | tf_op jit(solution)/shard_map/psum | solution.py:148
  (680 shorter events, 269.6 us)
Async XLA Ops:
  7.2 502.7 %copy-start = (bf16[512,1024]{1,0:T(8,128)(2,1)S(1)}, bf16[512,1024]{1,0:T(8,128)(2,1)}, u32[]{:S(2)}) copy-start(bf16[512,1024]{1,0:T(8,128)(2,1)} %param.21) | copy-start | bytes 3145732
  7.2 280.6 %all-gather.6.cloned.1.call-start = ((), (), s32[]{:S(2)}) async-start(), calls=%async_computation.2 | async-start | bytes 8650752 | tf_op jit(solution)/shard_map/all_gather | solution.py:13
  227.6 0.7 copy-start.1
  228.3 279.9 %all-reduce.3.cloned.1.call-start = ((), (), s32[]{:S(2)}) async-start(), calls=%async_computation | async-start | bytes 131072 | tf_op jit(solution)/shard_map/psum | solution.py:136
  315.6 119.5 %copy-start.3 = (bf16[128,1024]{1,0:T(8,128)(2,1)S(1)}, bf16[128,1024]{1,0:T(8,128)(2,1)}, u32[]{:S(2)}) copy-start(bf16[128,1024]{1,0:T(8,128)(2,1)} %param.18) | copy-start | bytes 786436
  315.7 192.6 %copy-start.2 = (bf16[16,1024]{1,0:T(8,128)(2,1)S(1)}, bf16[16,1024]{1,0:T(8,128)(2,1)}, u32[]{:S(2)}) copy-start(bf16[16,1024]{1,0:T(8,128)(2,1)} %param.15) | copy-start | bytes 98308
  315.7 193.5 %copy-start.4 = (f32[1024]{0:T(1024)S(1)}, f32[1024]{0:T(1024)}, u32[]{:S(2)}) copy-start(f32[1024]{0:T(1024)} %param.19) | copy-start | bytes 12292
  436.0 145.8 %all-reduce.5.cloned.1.call-start = ((), (), s32[]{:S(2)}) async-start(), calls=%async_computation.1 | async-start | bytes 131072 | tf_op jit(solution)/shard_map/psum | solution.py:148
Sparse Core Ops, SparseCore 0:
  228.4 59.3 all-gather.5
  436.1 72.0 all-reduce.2
  510.9 70.8 all-reduce.4
where the time goes:
time: 593 us; the launch traced here: 590 us
  local copies, waits for them, and re-layouts  206 us (35%)
  waiting for transfers between devices  148 us (25%)
  other arithmetic  126 us (21%)
  blocking collectives  72.1 us (12%)
  matrix products  20.3 us (3%)
  between operations  13.9 us (2%)
    add x31, other arithmetic, combine(): first[2] * shrink_first[:, :, None] + second[2] * shrink_second[:, :, None]  108 us
    psum x1, waiting for transfers between devices, body(): lax.psum(jnp.dot(activated, w_down, preferred_element_type=jnp.float32),...  70.4 us
    psum x1, waiting for transfers between devices, body(): lax.psum(jnp.dot(context, w_out, preferred_element_type=jnp.float32), 'mp')  65.8 us
    gather x16, local copies, waits for them, and re-layouts, visit(): fetched = jnp.take(kv_cache, picked, axis=1)  64.4 us
    all_gather x2, blocking collectives, merged_2(): pieces = jax.tree.map(lambda part: lax.all_gather(part, axis), value)  47.4 us
    all_gather x1, blocking collectives, body(): every_query = lax.all_gather(projected[:, 0], 'dp', axis=0, tiled=True)  24.7 us
    gather x16, local copies, waits for them, and re-layouts, visit(): usable = (owners[:, None] >= 0) & (position < lengths[clamped][:, None])  21.2 us
    gather x16, local copies, waits for them, and re-layouts, visit(): owners = page_request[picked]  20.8 us
  transfers between devices with their start and end apart: 3, of which 3 were waited for; matrix products, arithmetic and copies ran while one was open for 1% of the time, Pallas kernels for 0%

commit v1 on v0

--- a/solution.py
+++ b/solution.py
@@ -145,7 +145,9 @@
         preferred_element_type=jnp.float32,
     ).reshape(local_rows, 2, hidden_cols)
     activated = (jax.nn.silu(gate_up[:, 0]) * gate_up[:, 1]).astype(jnp.bfloat16)
-    lowered = lax.psum(jnp.dot(activated, w_down, preferred_element_type=jnp.float32), "mp")
+    lowered = jnp.sum(
+        lax.all_gather(jnp.dot(activated, w_down, preferred_element_type=jnp.float32), "mp"), axis=0
+    )
     hidden_out = (residual.astype(jnp.float32) + lowered).astype(jnp.bfloat16)
     return (appended, hidden_out)
 

time: 593 us -> 548 us (0.924)
  waiting for transfers between devices: 148 us -> 78.9 us
  blocking collectives: 72.1 us -> 97.4 us
    psum x1 -> x0, waiting for transfers between devices: 70.4 us -> none  [body(): lax.psum(jnp.dot(activated, w_down, preferred_element_type=jnp.float32),...]
    all_gather x0 -> x1, blocking collectives: none -> 25.3 us  [body(): lax.all_gather(jnp.dot(activated, w_down, preferred_element_type=jnp.floa...]
  transfers between devices with their start and end apart: 3 -> 2, of which waited for: 3 -> 2; matrix products, arithmetic and copies ran while one was open for 1% -> 1% of each run, Pallas kernels for 0% -> 0%
where the time goes in v1:
time: 548 us; the launch traced here: 544 us
  local copies, waits for them, and re-layouts  205 us (37%)
  other arithmetic  125 us (23%)
  blocking collectives  97.4 us (18%)
  waiting for transfers between devices  78.9 us (14%)
  matrix products  21.3 us (4%)
  between operations  14.2 us (3%)
    add x31, other arithmetic, combine(): first[2] * shrink_first[:, :, None] + second[2] * shrink_second[:, :, None]  108 us
    psum x1, waiting for transfers between devices, body(): lax.psum(jnp.dot(context, w_out, preferred_element_type=jnp.float32), 'mp')  71.6 us
    gather x16, local copies, waits for them, and re-layouts, visit(): fetched = jnp.take(kv_cache, picked, axis=1)  64.4 us
    all_gather x2, blocking collectives, merged_2(): pieces = jax.tree.map(lambda part: lax.all_gather(part, axis), value)  47.4 us
    all_gather x1, blocking collectives, body(): lax.all_gather(jnp.dot(activated, w_down, preferred_element_type=jnp.floa...  25.3 us
    all_gather x1, blocking collectives, body(): every_query = lax.all_gather(projected[:, 0], 'dp', axis=0, tiled=True)  24.7 us
    gather x16, local copies, waits for them, and re-layouts, visit(): usable = (owners[:, None] >= 0) & (position < lengths[clamped][:, None])  21.2 us
    gather x16, local copies, waits for them, and re-layouts, visit(): owners = page_request[picked]  20.8 us
  transfers between devices with their start and end apart: 2, of which 2 were waited for; matrix products, arithmetic and copies ran while one was open for 1% of the time, Pallas kernels for 0%

profile of v1, /device:TPU:2, one launch (start us, length us, event | category | flops | bytes accessed | tf_op | source)
XLA Modules:
  0.0 544.5 jit_solution(3065400921297633124)
XLA Ops:
  11.2 24.7 %all-gather = bf16[512,1,128]{2,0,1:T(8,128)(2,1)S(1)} all-gather(bf16[16,1,128]{2,0,1:T(8,128)(2,1)S(1)} %copy.113), channel_id=2, replica_groups=mesh['dp'=32,'mp'=8] {'dp'}, dimensions={0}, use_global_device_ids=true | all-gather | bytes 135168 | tf_op jit(solution)/shard_map/all_gather | solution.py:64
  36.7 190.9 %while.35 = (s32[]{:T(128)}, f32[512,2]{0,1:T(2,128)S(1)}, f32[512,2]{0,1:T(2,128)S(1)}, f32[512,2,64]{0,2,1:T(8,128)S(1)}, s32[128]{0:T(128)S(1)}, /*index=5*/s...) while((s32[]{:T(128)}, f32[512,2]{0,1:T(2,128)S(1)}, ...), condition=%wide.region_6.7_spmd.clone.clone, body=%wide.region_2.6_spmd.clone.clone.sunk | while | flops 7361630 | bytes 5361311 | solution.py:127
  41.5 4.0 gather_fusion.2
  53.5 4.0 gather_fusion.2
  65.4 4.0 gather_fusion.2
  77.3 4.0 gather_fusion.2
  89.3 4.0 gather_fusion.2
  101.2 4.0 gather_fusion.2
  113.1 4.0 gather_fusion.2
  125.1 4.0 gather_fusion.2
  137.0 4.0 gather_fusion.2
  148.9 4.0 gather_fusion.2
  160.9 4.0 gather_fusion.2
  172.8 4.0 gather_fusion.2
  184.7 4.0 gather_fusion.2
  220.5 4.0 gather_fusion.2
  228.4 22.8 %all-gather.1 = f32[16384,2]{0,1:T(2,128)S(1)} all-gather(f32[512,2]{0,1:T(2,128)S(1)} %get-tuple-element.259), channel_id=3, replica_groups=mesh['dp'=32,'mp'=8] {'dp'}, dimensions={0}, use_global_device_ids=true | all-gather | bytes 135168 | tf_op jit(solution)/shard_map/all_gather | solution.py:13
  251.2 24.6 %all-gather.2 = f32[16384,2]{0,1:T(2,128)S(1)} all-gather(f32[512,2]{0,1:T(2,128)S(1)} %get-tuple-element.260), channel_id=4, replica_groups=mesh['dp'=32,'mp'=8] {'dp'}, dimensions={0}, use_global_device_ids=true | all-gather | bytes 135168 | tf_op jit(solution)/shard_map/all_gather | solution.py:13
  280.6 7.2 %all-gather.7.cloned.1.call-done = f32[16384,2,64]{0,2,1:T(8,128)} async-done(((f32[512,2,64]{0,2,1:T(8,128)}), f32[16384,2,64]{0,2,1:T(8,128)}) %all-gather.7.cloned.1.call-update) | async-done | bytes 8388624 | tf_op jit(solution)/shard_map/all_gather | solution.py:13
  289.0 7.1 %slice.95 = f32[15872,2,64]{0,2,1:T(8,128)} slice(f32[16384,2,64]{0,2,1:T(8,128)} %all-gather.7.cloned.1.call-done), slice={[512:16384], [0:2], [0:64]} | slice | bytes 16252928 | tf_op jit(solution)/shard_map/slice | solution.py:15
  296.1 19.6 %copy.125 = f32[15872,2,64]{2,1,0:T(2,128)} copy(f32[15872,2,64]{0,2,1:T(8,128)} %slice.95) | data formatting | bytes 16252928 | tf_op jit(solution)/shard_map/while | solution.py:16
  315.7 119.1 %while.34 = (s32[]{:T(128)}, f32[512,2]{0,1:T(2,128)S(1)}, f32[512,2]{0,1:T(2,128)S(1)}, f32[512,2,64]{2,1,0:T(2,128)S(1)}, f32[31,512,2]{1,2,0:T(2,128)S(1)}, /...) while((s32[]{:T(128)}, f32[512,2]{0,1:T(2,128)S(1)}, f32[512,2]{0,1:T(2,128)S(1)}, ...), condition=%wide.region_8.9_spmd, body=%wide.region_7.8_spmd.sunk | while | flops 202754 | bytes 843877 | solution.py:16
  436.6 71.6 %all-reduce.2.cloned.1.call-done = f32[16,1024]{1,0:T(8,128)} async-done(((f32[16,1024]{1,0:T(8,128)}), f32[16,1024]{1,0:T(8,128)}) %all-reduce.2.cloned.1.call-update) | async-done | bytes 65552 | tf_op jit(solution)/shard_map/psum | solution.py:136
  511.7 25.3 %all-gather.4 = f32[128,1024]{1,0:T(8,128)S(1)} all-gather(f32[16,1024]{1,0:T(8,128)S(1)} %fusion.35), channel_id=6, replica_groups=mesh['dp'=32,'mp'=8] {'mp'}, dimensions={0}, use_global_device_ids=true | all-gather | bytes 589824 | tf_op jit(solution)/shard_map/all_gather | solution.py:149
  (679 shorter events, 268.1 us)
Async XLA Ops:
  7.2 504.3 %copy-start = (bf16[512,1024]{1,0:T(8,128)(2,1)S(1)}, bf16[512,1024]{1,0:T(8,128)(2,1)}, u32[]{:S(2)}) copy-start(bf16[512,1024]{1,0:T(8,128)(2,1)} %param.21) | copy-start | bytes 3145732
  7.2 280.6 %all-gather.7.cloned.1.call-start = ((), (), s32[]{:S(2)}) async-start(), calls=%async_computation.1 | async-start | bytes 8650752 | tf_op jit(solution)/shard_map/all_gather | solution.py:13
  227.6 0.7 copy-start.1
  228.3 279.9 %all-reduce.2.cloned.1.call-start = ((), (), s32[]{:S(2)}) async-start(), calls=%async_computation | async-start | bytes 131072 | tf_op jit(solution)/shard_map/psum | solution.py:136
  315.6 119.5 %copy-start.3 = (bf16[128,1024]{1,0:T(8,128)(2,1)S(1)}, bf16[128,1024]{1,0:T(8,128)(2,1)}, u32[]{:S(2)}) copy-start(bf16[128,1024]{1,0:T(8,128)(2,1)} %param.18) | copy-start | bytes 786436
  315.7 192.6 %copy-start.2 = (bf16[16,1024]{1,0:T(8,128)(2,1)S(1)}, bf16[16,1024]{1,0:T(8,128)(2,1)}, u32[]{:S(2)}) copy-start(bf16[16,1024]{1,0:T(8,128)(2,1)} %param.15) | copy-start | bytes 98308
  315.7 193.5 %copy-start.4 = (f32[1024]{0:T(1024)S(1)}, f32[1024]{0:T(1024)}, u32[]{:S(2)}) copy-start(f32[1024]{0:T(1024)} %param.19) | copy-start | bytes 12292
Sparse Core Ops, SparseCore 0:
  228.4 59.3 all-gather.6
  436.1 72.0 all-reduce.1
